TPU v7x, 32 devices: a whole 2x2x4 slice. The times are simulated.
32 devices in a mesh: group: 4 (over z), member: 8 (over y, x, core).
Axes of the slice: x: 2, y: 2, z: 4, core: 2. Of those that a mesh axis runs over, the one named last changes fastest.
Arguments:
- query_feat: bfloat16 [4096, 4096], P(('group', 'member'))
- code_feat: bfloat16 [4096, 4096], P(('group', 'member'))
- projection: bfloat16 [4096, 1024], replicated
- hard_ids: int32 [32, 16], P(('group', 'member')), may hold values from 0 to 63, as said below
- loss_weight: float32 [4096], P(('group', 'member')), may hold values from 1 to 4
Outputs:
- query_grad: bfloat16 [4096, 4096], P(('group', 'member'))
- code_grad: bfloat16 [4096, 4096], P(('group', 'member'))
- projection_grad: float32 [4096, 1024], P(('group', 'member'))
Inputs may be any that keep to these rules, and one draw needn't show every extreme that they name: `hard_ids`: entry (owner device g * 8 + m) * 2 + slot names code rows of that device. A row names 16 different blocks, none of its own group; at most 8 of them lie in one group, and exactly 8 in some group of every row.
All inputs are finite; a program needn't handle non-finite values.
Results may differ from a plain program's by a relative error of at most 0.02.
Values may be sent and summed in bfloat16 or wider, within the bound.
No kernel may reach another device: no remote copies, remote signals or barrier semaphores. Data moves between devices by JAX's collectives and lax.ppermute only.
A program may use at most 128 MiB of HBM per device.

v0:
```python
import jax
import jax.numpy as jnp
from jax import lax
from jax.sharding import PartitionSpec as P

CB = 64
inverse_temp = 120.0
epsilon = 1e-06


def embed(features, projection):
    values = jnp.dot(features, projection, preferred_element_type=jnp.float32)
    inverse = lax.rsqrt(jnp.sum(values * values, axis=1) + epsilon)
    unit_vec = values * inverse[:, None]
    return (unit_vec, inverse, unit_vec.astype(jnp.bfloat16))


def norm_back(upstream, unit_vec, inverse):
    inner_prod = jnp.sum(unit_vec * upstream, axis=1, keepdims=True)
    return (inverse[:, None] * (upstream - unit_vec * inner_prod)).astype(jnp.bfloat16)


def body(query_feat, code_feat, projection, hard_ids, loss_weight):
    groups = lax.axis_size("group")
    members = lax.axis_size("member")
    group_index = lax.axis_index("group")
    member_index = lax.axis_index("member")
    queries_dev = query_feat.shape[0]
    feat_width = query_feat.shape[1]
    emb_width = projection.shape[1]
    slot_count = queries_dev // CB
    per_group = members * slot_count
    group_span = members * queries_dev
    rows_dev = feat_width // (groups * members)
    feats = jnp.stack([query_feat, code_feat], axis=0).reshape(
        2, queries_dev, groups, members, rows_dev
    )
    feats = jnp.transpose(feats, (3, 0, 1, 2, 4))
    feat_cols = lax.all_to_all(feats, "member", split_axis=0, concat_axis=0, tiled=True)
    q_unit, q_inv, q_emb = embed(query_feat, projection)
    c_unit, c_inv, c_emb = embed(code_feat, projection)
    group_codes = lax.all_gather(c_emb, "member", axis=0, tiled=True)
    q_all = lax.all_gather(q_emb, "group", axis=0)
    ids_all = lax.all_gather(hard_ids[0], "group", axis=0)
    w_all = lax.all_gather(loss_weight, "group", axis=0)
    block_ids = group_index * per_group + jnp.arange(per_group, dtype=jnp.int32)
    asked = jnp.any(ids_all[:, :, None] == block_ids[None, None, :], axis=1)
    own = jnp.arange(groups, dtype=jnp.int32) == group_index
    block_mask = asked | own[:, None]
    col_mask = jnp.broadcast_to(block_mask[:, :, None], (groups, per_group, CB)).reshape(
        groups, 1, group_span
    )
    scores = inverse_temp * jnp.einsum(
        "gqe,ke->gqk", q_all, group_codes, preferred_element_type=jnp.float32
    )
    scores = jnp.where(col_mask, scores, -jnp.inf)
    part_max = jnp.max(scores, axis=2)
    safe_max = jnp.where(part_max > -jnp.inf, part_max, 0.0)
    part_sum = jnp.sum(jnp.exp(scores - safe_max[:, :, None]), axis=2)
    stats = lax.all_gather(jnp.stack([part_max, part_sum], axis=0), "group", axis=0)
    row_max = jnp.max(stats[:, 0], axis=0)
    row_sum = jnp.sum(stats[:, 1] * jnp.exp(stats[:, 0] - row_max[None]), axis=0)
    log_total = row_max + jnp.log(row_sum)
    offsets = jnp.arange(queries_dev, dtype=jnp.int32)
    columns = jnp.arange(group_span, dtype=jnp.int32)
    positive = (columns[None, :] == (member_index * queries_dev + offsets)[:, None]).astype(
        jnp.float32
    )
    positive = positive[None] * own[:, None, None].astype(jnp.float32)
    factor = w_all * inverse_temp
    grad = (factor[:, :, None] * (jnp.exp(scores - log_total[:, :, None]) - positive)).astype(
        jnp.bfloat16
    )
    delta_parts = jnp.einsum("gqk,ke->gqe", grad, group_codes, preferred_element_type=jnp.float32)
    query_delta = lax.psum_scatter(delta_parts, "group", scatter_dimension=0, tiled=True).reshape(
        queries_dev, emb_width
    )
    code_terms = None
    for g in range(groups):
        term = jnp.dot(grad[g].T, q_all[g], preferred_element_type=jnp.float32)
        term = jnp.where(g == group_index, term, term.astype(jnp.bfloat16).astype(jnp.float32))
        code_terms = term if code_terms is None else code_terms + term
    code_delta = lax.psum_scatter(
        code_terms.astype(jnp.bfloat16), "member", scatter_dimension=0, tiled=True
    ).astype(jnp.float32)
    dz_query = norm_back(query_delta, q_unit, q_inv)
    dz_code = norm_back(code_delta, c_unit, c_inv)
    query_grad = jnp.einsum(
        "qe,de->qd", dz_query, projection, preferred_element_type=jnp.float32
    ).astype(jnp.bfloat16)
    code_grad = jnp.einsum(
        "qe,de->qd", dz_code, projection, preferred_element_type=jnp.float32
    ).astype(jnp.bfloat16)
    dz_all = lax.all_gather(jnp.stack([dz_query, dz_code], axis=0), "member", axis=0)
    proj_parts = jnp.einsum(
        "mtqgr,mtqe->gre", feat_cols, dz_all, preferred_element_type=jnp.float32
    )
    projection_grad = lax.psum_scatter(
        proj_parts, "group", scatter_dimension=0, tiled=True
    ).reshape(rows_dev, emb_width)
    return (query_grad, code_grad, projection_grad)


def solution(mesh):
    return jax.shard_map(
        body,
        mesh=mesh,
        in_specs=(
            P(("group", "member"), None),
            P(("group", "member"), None),
            P(),
            P(("group", "member"), None),
            P(("group", "member")),
        ),
        out_specs=(
            P(("group", "member"), None),
            P(("group", "member"), None),
            P(("group", "member"), None),
        ),
        check_vma=False,
    )
```

profile of v0, /device:TPU:0, one launch (start us, length us, event | category | flops | bytes accessed | tf_op | source)
XLA Modules:
  0.0 291.4 jit_solution(1036864795923591170)
XLA Ops:
  7.2 5.1 %multiply_reduce_fusion.1 = (f32[128]{0:T(128)S(1)}, f32[128,1024]{1,0:T(8,128)S(1)}) fusion(bf16[128,4096]{1,0:T(8,128)(2,1)} %param.5, bf16[4096,1024]{1,0:T(8,128)(2,1)} %param.7), kind=kOutput, calls=%fused_computation.25 | convolution fusion | flops 1074003840 | bytes 9961984 | tf_op jit(solution)/shard_map/dot_general | solution.py:12
  13.6 4.7 %multiply_reduce_fusion = (f32[128]{0:T(128)S(1)}, f32[128,1024]{1,0:T(8,128)S(1)}) fusion(bf16[128,4096]{1,0:T(8,128)(2,1)S(1)} %copy-done, bf16[4096,1024]{1,0:T(8,128)(2,1)} %param.7), kind=kOutput, calls=%fused_computation.24 | convolution fusion | flops 1074003840 | bytes 9961984 | tf_op jit(solution)/shard_map/dot_general | solution.py:12
  19.2 12.9 %all-gather.5 = s32[4,1,16]{2,1,0:T(1,128)S(1)} all-gather(s32[1,1,16]{2,1,0:T(1,128)S(1)} %bitcast.92), channel_id=1, replica_groups=mesh['group'=4,'member'=8] {'group'}, dimensions={0}, use_global_device_ids=true | all-gather | bytes 320 | tf_op jit(solution)/shard_map/all_gather | solution.py:44
  32.5 7.9 %all-gather.4 = f32[4,1,128]{2,1,0:T(1,128)S(1)} all-gather(f32[1,1,128]{2,1,0:T(1,128)S(1)} %bitcast.93), channel_id=2, replica_groups=mesh['group'=4,'member'=8] {'group'}, dimensions={0}, use_global_device_ids=true | all-gather | bytes 2560 | tf_op jit(solution)/shard_map/all_gather | solution.py:45
  40.4 0.9 fusion.12
  41.3 2.8 all-gather.12.cloned.1.call-done
  44.0 29.7 %all-gather.10.cloned.1.call-done = bf16[1024,1024]{1,0:T(8,128)(2,1)} async-done(((bf16[128,1024]{1,0:T(8,128)(2,1)}), bf16[1024,1024]{1,0:T(8,128)(2,1)}) %all-gather.10.cloned.1.call-update) | async-done | bytes 2097168 | tf_op jit(solution)/shard_map/all_gather | solution.py:42
  73.7 3.3 %fusion.24 = (f32[4,128]{1,0:T(4,128)S(1)}, f32[4,128,1024]{2,1,0:T(8,128)S(1)}) fusion(bf16[4,128,1024]{2,1,0:T(8,128)(2,1)} %bitcast.85, bf16[1024,1024]{1,0:T(8,128)(2,1)} %all-gather.10.cloned.1.call-done, pred[4,1024]{1,0:T(4,128)(4,1)S(1)} %broadcast_in_dim.21), kind=kOutput, calls=%fused_computation.58 | convolution fusion | flops 1075314176 | bytes 5249024 | tf_op jit(solution)/shard_map/gqe,ke->gqk/dot_general | solution.py:53
  77.5 13.4 %all-gather.2 = f32[8,4,128]{2,1,0:T(4,128)S(1)} all-gather(f32[2,4,128]{2,1,0:T(4,128)S(1)} %pad_maximum_fusion.1), channel_id=4, replica_groups=mesh['group'=4,'member'=8] {'group'}, dimensions={0}, use_global_device_ids=true | all-gather | bytes 20480 | tf_op jit(solution)/shard_map/all_gather | solution.py:60
  93.8 2.4 add_convert_fusion
  96.3 4.1 %fusion = f32[4,128,1024]{2,1,0:T(8,128)} fusion(bf16[4,128,1024]{2,1,0:T(8,128)(2,1)S(1)} %multiply_convert_fusion, bf16[1024,1024]{1,0:T(8,128)(2,1)} %all-gather.10.cloned.1.call-done), kind=kOutput, calls=%fused_computation.4 | convolution fusion | flops 1073741824 | bytes 5242880 | tf_op jit(solution)/shard_map/gqk,ke->gqe/dot_general | solution.py:74
  100.5 37.0 %reduce-scatter.6.cloned.1.call-done = bf16[128,1024]{1,0:T(8,128)(2,1)} async-done(((bf16[1024,1024]{1,0:T(8,128)(2,1)}), bf16[128,1024]{1,0:T(8,128)(2,1)}) %reduce-scatter.6.cloned.1.call-update) | async-done | bytes 262160 | tf_op jit(solution)/shard_map/reduce_scatter | solution.py:83
  137.4 1.2 fusion.6
  138.6 1.1 fusion.8
  139.7 43.5 %reduce-scatter.4.cloned.1.call-done = f32[1,128,1024]{2,1,0:T(8,128)} async-done(((f32[4,128,1024]{2,1,0:T(8,128)}), f32[1,128,1024]{2,1,0:T(8,128)}) %reduce-scatter.4.cloned.1.call-update) | async-done | bytes 524304 | tf_op jit(solution)/shard_map/reduce_scatter | solution.py:75
  183.2 1.2 fusion.9
  184.5 1.2 fusion.11
  185.7 0.8 pad_maximum_fusion
  188.3 38.3 %all_to_all.5 = bf16[8,2,128,4,128]{2,4,1,3,0:T(8,128)(2,1)} all-to-all(bf16[8,2,128,4,128]{2,4,1,3,0:T(8,128)(2,1)S(1)} %copy.20), channel_id=1, replica_groups=mesh['group'=4,'member'=8] {'member'}, dimensions={0} | all-to-all | bytes 4194304 | tf_op jit(solution)/shard_map/all_to_all | solution.py:39
  226.6 9.4 %all-gather.14.cloned.1.call-done = bf16[16,128,1024]{2,1,0:T(8,128)(2,1)} async-done(((bf16[2,128,1024]{2,1,0:T(8,128)(2,1)}), bf16[16,128,1024]{2,1,0:T(8,128)(2,1)}) %all-gather.14.cloned.1.call-update) | async-done | bytes 4194320 | tf_op jit(solution)/shard_map/all_gather | solution.py:94
  236.0 6.5 %convolution_bitcast_fusion = f32[4,128,1024]{2,1,0:T(8,128)} fusion(bf16[8,2,128,4,128]{2,4,1,3,0:T(8,128)(2,1)} %all_to_all.5, bf16[8,2,128,1024,1]{3,2,1,4,0:T(8,128)(2,1)} %bitcast.94), kind=kOutput, calls=%fused_computation.11 | convolution fusion | flops 2147483648 | bytes 8388608 | tf_op jit(solution)/shard_map/mtqgr,mtqe->gre/dot_general | solution.py:95
  242.5 7.3 %convolution_convert_fusion = bf16[128,4096]{1,0:T(8,128)(2,1)} fusion(bf16[128,1024]{1,0:T(8,128)(2,1)S(1)} %fusion.8, bf16[4096,1024]{1,0:T(8,128)(2,1)} %param.7), kind=kOutput, calls=%fused_computation | convolution fusion | flops 1074266112 | bytes 9699328 | tf_op jit(solution)/shard_map/qe,de->qd/dot_general | solution.py:91
  249.8 7.2 %convolution_convert_fusion.1 = bf16[128,4096]{1,0:T(8,128)(2,1)} fusion(bf16[128,1024]{1,0:T(8,128)(2,1)S(1)} %copy-done.3, bf16[4096,1024]{1,0:T(8,128)(2,1)} %param.7), kind=kOutput, calls=%fused_computation.1 | convolution fusion | flops 1074266112 | bytes 9699328 | tf_op jit(solution)/shard_map/qe,de->qd/dot_general | solution.py:88
  257.0 27.5 %reduce-scatter.8.cloned.1.call-done = f32[1,128,1024]{2,1,0:T(8,128)} async-done(((f32[4,128,1024]{2,1,0:T(8,128)}), f32[1,128,1024]{2,1,0:T(8,128)}) %reduce-scatter.8.cloned.1.call-update) | async-done | bytes 524304 | tf_op jit(solution)/shard_map/reduce_scatter | solution.py:98
  (55 shorter events, 7.8 us)
Async XLA Ops:
  7.2 36.9 %all-gather.12.cloned.1.call-start = ((), (), s32[]{:S(2)}) async-start(), calls=%async_computation.8 | async-start | bytes 1310720 | tf_op jit(solution)/shard_map/all_gather | solution.py:43
  12.3 1.3 copy-start
  13.1 6.1 %copy-start.6 = (s32[1,16]{1,0:T(1,128)S(1)}, s32[1,16]{1,0:T(1,128)}, u32[]{:S(2)}) copy-start(s32[1,16]{1,0:T(1,128)} %param.8) | copy-start | bytes 196
  13.1 19.4 %copy-start.7 = (f32[128]{0:T(128)S(1)}, f32[128]{0:T(128)}, u32[]{:S(2)}) copy-start(f32[128]{0:T(128)} %param.9) | copy-start | bytes 1540
  13.1 60.5 %all-gather.10.cloned.1.call-start = ((), (), s32[]{:S(2)}) async-start(), calls=%async_computation.4 | async-start | bytes 2359296 | tf_op jit(solution)/shard_map/all_gather | solution.py:42
  19.2 118.3 %reduce-scatter.6.cloned.1.call-start = ((), (), s32[]{:S(2)}) async-start(), calls=%async_computation.6 | async-start | bytes 2359296 | tf_op jit(solution)/shard_map/reduce_scatter | solution.py:83
  77.0 14.0 %copy-start.4 = (f32[128,1024]{1,0:T(8,128)S(1)}, f32[128,1024]{1,0:T(8,128)}, u32[]{:S(2)}) copy-start(f32[128,1024]{1,0:T(8,128)} %fusion.12) | copy-start | bytes 1572868
  77.5 14.1 %copy-start.5 = (bf16[512,1024]{1,0:T(8,128)(2,1)S(1)}, bf16[512,1024]{1,0:T(8,128)(2,1)}, u32[]{:S(2)}) copy-start(bf16[512,1024]{1,0:T(8,128)(2,1)} %all-gather.12.cloned.1.call-done) | copy-start | bytes 3145732
  96.2 87.0 %reduce-scatter.4.cloned.1.call-start = ((), (), s32[]{:S(2)}) async-start(), calls=%async_computation.5 | async-start | bytes 2621440 | tf_op jit(solution)/shard_map/reduce_scatter | solution.py:75
  100.4 135.6 %all-gather.14.cloned.1.call-start = ((), (), s32[]{:S(2)}) async-start(), calls=%async_computation.9 | async-start | bytes 4718592 | tf_op jit(solution)/shard_map/all_gather | solution.py:94
  185.7 0.9 copy-start.2
  185.7 1.6 copy-start.1
  186.6 98.0 %reduce-scatter.8.cloned.1.call-start = ((), (), s32[]{:S(2)}) async-start(), calls=%async_computation.7 | async-start | bytes 2621440 | tf_op jit(solution)/shard_map/reduce_scatter | solution.py:98
  242.5 7.3 %copy-start.3 = (bf16[128,1024]{1,0:T(8,128)(2,1)S(1)}, bf16[128,1024]{1,0:T(8,128)(2,1)}, u32[]{:S(2)}) copy-start(bf16[128,1024]{1,0:T(8,128)(2,1)} %copy-done.2) | copy-start | bytes 786436
Sparse Core Ops, SparseCore 0:
  13.2 30.7 all-gather.11
  46.5 27.1 all-gather.9
  96.3 41.0 reduce-scatter.5
  139.6 43.5 reduce-scatter.3
  186.7 49.2 all-gather.13
  242.6 41.9 reduce-scatter.7
where the time goes:
time: 292 us; the launch traced here: 291 us
  waiting for transfers between devices  150 us (51%)
  blocking collectives  72.5 us (25%)
  matrix products  42.8 us (15%)
  between operations  14.3 us (5%)
  other arithmetic  9.61 us (3%)
    reduce_scatter x1, waiting for transfers between devices, body(): lax.psum_scatter(delta_parts, 'group', scatter_dimension=0, tiled=True)  43.5 us
    all_to_all x1, blocking collectives, body(): lax.all_to_all(feats, 'member', split_axis=0, concat_axis=0, tiled=True)  38.3 us
    reduce_scatter x1, waiting for transfers between devices, body(): lax.psum_scatter(code_terms.astype(jnp.bfloat16), 'member', scatter_dimen...  37 us
    all_gather x1, waiting for transfers between devices, body(): group_codes = lax.all_gather(c_emb, 'member', axis=0, tiled=True)  29.7 us
    reduce_scatter x1, waiting for transfers between devices, body(): lax.psum_scatter(proj_parts, 'group', scatter_dimension=0, tiled=True)  27.5 us
    all_gather x1, blocking collectives, body(): lax.all_gather(jnp.stack([part_max, part_sum], axis=0), 'group', axis=0)  13.4 us
    all_gather x1, blocking collectives, body(): ids_all = lax.all_gather(hard_ids[0], 'group', axis=0)  12.9 us
    dot_general x2, matrix products, embed(): values = jnp.dot(features, projection, preferred_element_type=jnp.float32)  9.78 us
  transfers between devices with their start and end apart: 6, of which 6 were waited for; matrix products, arithmetic and copies ran while one was open for 10% of the time, Pallas kernels for 0%

commit v1 on v0

--- a/solution.py
+++ b/solution.py
@@ -6,6 +6,12 @@
 CB = 64
 inverse_temp = 120.0
 epsilon = 1e-06
+
+
+def derive_strips_all(own_rows, dimension_no):
+    earlier = list(own_rows.shape[1:])
+    earlier[dimension_no] *= own_rows.shape[0]
+    return jnp.moveaxis(own_rows, 0, dimension_no).reshape(earlier)
 
 
 def embed(features, projection):
@@ -39,7 +45,15 @@
     feat_cols = lax.all_to_all(feats, "member", split_axis=0, concat_axis=0, tiled=True)
     q_unit, q_inv, q_emb = embed(query_feat, projection)
     c_unit, c_inv, c_emb = embed(code_feat, projection)
-    group_codes = lax.all_gather(c_emb, "member", axis=0, tiled=True)
+    world = lax.axis_size("member")
+    log = [c_emb]
+    arrivals = tuple(((at, (at + 1) % world) for at in range(world)))
+    while len(log) < world:
+        log.append(lax.ppermute(log[-1], "member", arrivals))
+    side_arr = lax.axis_index("member")
+    now = jnp.stack(log, 0)
+    log = now[(side_arr - jnp.arange(world)) % world]
+    group_codes = derive_strips_all(log, 0)
     q_all = lax.all_gather(q_emb, "group", axis=0)
     ids_all = lax.all_gather(hard_ids[0], "group", axis=0)
     w_all = lax.all_gather(loss_weight, "group", axis=0)

time: 292 us -> 295 us (1.010)
  local copies, waits for them, and re-layouts: 2.08 us -> 11.5 us
  waiting for transfers between devices: 150 us -> 144 us
    all_gather x1 -> x0, waiting for transfers between devices: 29.7 us -> none  [body(): group_codes = lax.all_gather(c_emb, 'member', axis=0, tiled=True)]
    ppermute x0 -> x7, waiting for transfers between devices: none -> 27.9 us  [body(): log.append(lax.ppermute(log[-1], 'member', arrivals))]
    unnamed x18 -> x24, local copies, waits for them, and re-layouts: 1.77 us -> 6.81 us
    gather x0 -> x1, local copies, waits for them, and re-layouts: none -> 3.62 us  [body(): log = now[(side_arr - jnp.arange(world)) % world]]
  transfers between devices with their start and end apart: 6 -> 12, of which waited for: 6 -> 9; matrix products, arithmetic and copies ran while one was open for 10% -> 13% of each run, Pallas kernels for 0% -> 0%
where the time goes in v1:
time: 295 us
  waiting for transfers between devices  144 us (49%)
  blocking collectives  71.8 us (24%)
  matrix products  42.8 us (15%)
  between operations  14 us (5%)
  local copies, waits for them, and re-layouts  11.5 us (4%)
  other arithmetic  9.66 us (3%)
    reduce_scatter x1, waiting for transfers between devices, body(): lax.psum_scatter(delta_parts, 'group', scatter_dimension=0, tiled=True)  43.6 us
    all_to_all x1, blocking collectives, body(): lax.all_to_all(feats, 'member', split_axis=0, concat_axis=0, tiled=True)  38.3 us
    reduce_scatter x1, waiting for transfers between devices, body(): lax.psum_scatter(code_terms.astype(jnp.bfloat16), 'member', scatter_dimen...  35.6 us
    ppermute x7, waiting for transfers between devices, body(): log.append(lax.ppermute(log[-1], 'member', arrivals))  27.9 us
    reduce_scatter x1, waiting for transfers between devices, body(): lax.psum_scatter(proj_parts, 'group', scatter_dimension=0, tiled=True)  27.5 us
    all_gather x1, blocking collectives, body(): lax.all_gather(jnp.stack([part_max, part_sum], axis=0), 'group', axis=0)  13.3 us
    all_gather x1, blocking collectives, body(): ids_all = lax.all_gather(hard_ids[0], 'group', axis=0)  12.4 us
    dot_general x2, matrix products, embed(): values = jnp.dot(features, projection, preferred_element_type=jnp.float32)  9.78 us
  transfers between devices with their start and end apart: 12, of which 9 were waited for; matrix products, arithmetic and copies ran while one was open for 13% of the time, Pallas kernels for 0%

profile of v1, /device:TPU:0, one launch (start us, length us, event | category | flops | bytes accessed | tf_op | source)
XLA Modules:
  0.0 294.7 jit_solution(6427498882713667361)
XLA Ops:
  7.2 5.1 %multiply_reduce_fusion.1 = (f32[128]{0:T(128)S(1)}, f32[128,1024]{1,0:T(8,128)S(1)}) fusion(bf16[128,4096]{1,0:T(8,128)(2,1)} %param.5, bf16[4096,1024]{1,0:T(8,128)(2,1)} %param.7), kind=kOutput, calls=%fused_computation.22 | convolution fusion | flops 1074003840 | bytes 9961984 | tf_op jit(solution)/shard_map/dot_general | solution.py:18
  13.6 4.7 %multiply_reduce_fusion = (f32[128]{0:T(128)S(1)}, f32[128,1024]{1,0:T(8,128)S(1)}) fusion(bf16[128,4096]{1,0:T(8,128)(2,1)S(1)} %copy-done, bf16[4096,1024]{1,0:T(8,128)(2,1)} %param.7), kind=kOutput, calls=%fused_computation.21 | convolution fusion | flops 1074003840 | bytes 9961984 | tf_op jit(solution)/shard_map/dot_general | solution.py:18
  19.7 12.4 %all-gather.5 = s32[4,1,16]{2,1,0:T(1,128)S(1)} all-gather(s32[1,1,16]{2,1,0:T(1,128)S(1)} %bitcast.108), channel_id=1, replica_groups=mesh['group'=4,'member'=8] {'group'}, dimensions={0}, use_global_device_ids=true | all-gather | bytes 320 | tf_op jit(solution)/shard_map/all_gather | solution.py:58
  32.4 6.6 %collective-permute-done.1 = bf16[128,1024]{1,0:T(8,128)(2,1)S(1)} collective-permute-done((bf16[128,1024]{1,0:T(8,128)(2,1)S(1)}, bf16[128,1024]{1,0:T(8,128)(2,1)S(1)}, u32[]{:S(2)}, u32[]{:S(2)}) %collective-permute-start.1) | collective-permute-done | bytes 262176 | tf_op jit(solution)/shard_map/ppermute | solution.py:52
  39.0 7.7 %all-gather.4 = f32[4,1,128]{2,1,0:T(1,128)S(1)} all-gather(f32[1,1,128]{2,1,0:T(1,128)S(1)} %bitcast.109), channel_id=2, replica_groups=mesh['group'=4,'member'=8] {'group'}, dimensions={0}, use_global_device_ids=true | all-gather | bytes 2560 | tf_op jit(solution)/shard_map/all_gather | solution.py:59
  47.7 5.6 %collective-permute-done.3 = bf16[128,1024]{1,0:T(8,128)(2,1)S(1)} collective-permute-done((bf16[128,1024]{1,0:T(8,128)(2,1)S(1)}, bf16[128,1024]{1,0:T(8,128)(2,1)S(1)}, u32[]{:S(2)}, u32[]{:S(2)}) %collective-permute-start.3) | collective-permute-done | bytes 262176 | tf_op jit(solution)/shard_map/ppermute | solution.py:52
  54.8 5.3 %collective-permute-done.4 = bf16[128,1024]{1,0:T(8,128)(2,1)S(1)} collective-permute-done((bf16[128,1024]{1,0:T(8,128)(2,1)S(1)}, bf16[128,1024]{1,0:T(8,128)(2,1)S(1)}, u32[]{:S(2)}, u32[]{:S(2)}) %collective-permute-start.4) | collective-permute-done | bytes 262176 | tf_op jit(solution)/shard_map/ppermute | solution.py:52
  61.5 5.2 %collective-permute-done.5 = bf16[128,1024]{1,0:T(8,128)(2,1)S(1)} collective-permute-done((bf16[128,1024]{1,0:T(8,128)(2,1)S(1)}, bf16[128,1024]{1,0:T(8,128)(2,1)S(1)}, u32[]{:S(2)}, u32[]{:S(2)}) %collective-permute-start.5) | collective-permute-done | bytes 262176 | tf_op jit(solution)/shard_map/ppermute | solution.py:52
  68.2 5.2 %collective-permute-done.6 = bf16[128,1024]{1,0:T(8,128)(2,1)S(1)} collective-permute-done((bf16[128,1024]{1,0:T(8,128)(2,1)S(1)}, bf16[128,1024]{1,0:T(8,128)(2,1)S(1)}, u32[]{:S(2)}, u32[]{:S(2)}) %collective-permute-start.6) | collective-permute-done | bytes 262176 | tf_op jit(solution)/shard_map/ppermute | solution.py:52
  74.2 3.6 %gather_fusion = bf16[8,128,1024]{2,1,0:T(8,128)(2,1)} fusion(bf16[8,128,1024]{2,1,0:T(8,128)(2,1)} %bitcast_dynamic-update-slice_fusion, s32[1024]{0:T(1024)S(1)} %pad_clamp_fusion), kind=kCustom, calls=%fused_computation | custom fusion | bytes 4194336 | tf_op jit(solution)/shard_map/gather | solution.py:55
  77.8 3.3 %fusion.20 = (f32[4,128]{1,0:T(4,128)S(1)}, f32[4,128,1024]{2,1,0:T(8,128)S(1)}) fusion(bf16[4,128,1024]{2,1,0:T(8,128)(2,1)} %bitcast.101, bf16[1024,1024,1]{1,0,2:T(8,128)(2,1)} %bitcast.99, pred[4,1024]{1,0:T(4,128)(4,1)S(1)} %broadcast_in_dim.21), kind=kOutput, calls=%fused_computation.70 | convolution fusion | flops 1075314176 | bytes 5249024 | tf_op jit(solution)/shard_map/gqe,ke->gqk/dot_general | solution.py:67
  81.6 13.3 %all-gather.2 = f32[8,4,128]{2,1,0:T(4,128)S(1)} all-gather(f32[2,4,128]{2,1,0:T(4,128)S(1)} %pad_maximum_fusion.1), channel_id=4, replica_groups=mesh['group'=4,'member'=8] {'group'}, dimensions={0}, use_global_device_ids=true | all-gather | bytes 20480 | tf_op jit(solution)/shard_map/all_gather | solution.py:74
  97.9 2.4 add_convert_fusion
  100.3 4.1 %fusion.21 = f32[4,128,1024]{2,1,0:T(8,128)} fusion(bf16[4,128,1024]{2,1,0:T(8,128)(2,1)S(1)} %multiply_convert_fusion, bf16[1024,1024,1]{1,0,2:T(8,128)(2,1)} %bitcast.100), kind=kOutput, calls=%fused_computation.71 | convolution fusion | flops 1073741824 | bytes 5242880 | tf_op jit(solution)/shard_map/gqk,ke->gqe/dot_general | solution.py:88
  104.5 35.6 %reduce-scatter.6.cloned.1.call-done = bf16[128,1024]{1,0:T(8,128)(2,1)} async-done(((bf16[1024,1024]{1,0:T(8,128)(2,1)}), bf16[128,1024]{1,0:T(8,128)(2,1)}) %reduce-scatter.6.cloned.1.call-update) | async-done | bytes 262160 | tf_op jit(solution)/shard_map/reduce_scatter | solution.py:97
  142.5 43.6 %reduce-scatter.4.cloned.1.call-done = f32[1,128,1024]{2,1,0:T(8,128)} async-done(((f32[4,128,1024]{2,1,0:T(8,128)}), f32[1,128,1024]{2,1,0:T(8,128)}) %reduce-scatter.4.cloned.1.call-update) | async-done | bytes 524304 | tf_op jit(solution)/shard_map/reduce_scatter | solution.py:89
  186.1 1.2 fusion.3
  187.4 1.2 fusion.5
  191.9 38.3 %all_to_all.5 = bf16[8,2,128,4,128]{2,4,1,3,0:T(8,128)(2,1)} all-to-all(bf16[8,2,128,4,128]{2,4,1,3,0:T(8,128)(2,1)S(1)} %copy.20), channel_id=1, replica_groups=mesh['group'=4,'member'=8] {'member'}, dimensions={0} | all-to-all | bytes 4194304 | tf_op jit(solution)/shard_map/all_to_all | solution.py:45
  230.2 9.3 %all-gather.11.cloned.1.call-done = bf16[16,128,1024]{2,1,0:T(8,128)(2,1)} async-done(((bf16[2,128,1024]{2,1,0:T(8,128)(2,1)}), bf16[16,128,1024]{2,1,0:T(8,128)(2,1)}) %all-gather.11.cloned.1.call-update) | async-done | bytes 4194320 | tf_op jit(solution)/shard_map/all_gather | solution.py:108
  239.6 6.5 %convolution_bitcast_fusion = f32[4,128,1024]{2,1,0:T(8,128)} fusion(bf16[8,2,128,4,128]{2,4,1,3,0:T(8,128)(2,1)} %all_to_all.5, bf16[8,2,128,1024,1]{3,2,1,4,0:T(8,128)(2,1)} %bitcast.110), kind=kOutput, calls=%fused_computation.8 | convolution fusion | flops 2147483648 | bytes 8388608 | tf_op jit(solution)/shard_map/mtqgr,mtqe->gre/dot_general | solution.py:109
  246.1 7.3 %convolution_convert_fusion = bf16[128,4096]{1,0:T(8,128)(2,1)} fusion(bf16[128,1024]{1,0:T(8,128)(2,1)S(1)} %fusion.2, bf16[4096,1024]{1,0:T(8,128)(2,1)} %param.7), kind=kOutput, calls=%fused_computation.1 | convolution fusion | flops 1074266112 | bytes 9699328 | tf_op jit(solution)/shard_map/qe,de->qd/dot_general | solution.py:105
  253.4 7.2 %convolution_convert_fusion.1 = bf16[128,4096]{1,0:T(8,128)(2,1)} fusion(bf16[128,1024]{1,0:T(8,128)(2,1)S(1)} %copy-done.3, bf16[4096,1024]{1,0:T(8,128)(2,1)} %param.7), kind=kOutput, calls=%fused_computation.2 | convolution fusion | flops 1074266112 | bytes 9699328 | tf_op jit(solution)/shard_map/qe,de->qd/dot_general | solution.py:102
  260.6 27.5 %reduce-scatter.8.cloned.1.call-done = f32[1,128,1024]{2,1,0:T(8,128)} async-done(((f32[4,128,1024]{2,1,0:T(8,128)}), f32[1,128,1024]{2,1,0:T(8,128)}) %reduce-scatter.8.cloned.1.call-update) | async-done | bytes 524304 | tf_op jit(solution)/shard_map/reduce_scatter | solution.py:112
  (76 shorter events, 18.1 us)
Async XLA Ops:
  7.2 70.6 %all-gather.9.cloned.1.call-start = ((), (), s32[]{:S(2)}) async-start(), calls=%async_computation.7 | async-start | bytes 1310720 | tf_op jit(solution)/shard_map/all_gather | solution.py:57
  12.3 1.3 copy-start
  13.1 6.6 %copy-start.6 = (s32[1,16]{1,0:T(1,128)S(1)}, s32[1,16]{1,0:T(1,128)}, u32[]{:S(2)}) copy-start(s32[1,16]{1,0:T(1,128)} %param.8) | copy-start | bytes 196
  13.1 25.9 %copy-start.7 = (f32[128]{0:T(128)S(1)}, f32[128]{0:T(128)}, u32[]{:S(2)}) copy-start(f32[128]{0:T(128)} %param.9) | copy-start | bytes 1540
  13.1 127.0 %reduce-scatter.6.cloned.1.call-start = ((), (), s32[]{:S(2)}) async-start(), calls=%async_computation.5 | async-start | bytes 2359296 | tf_op jit(solution)/shard_map/reduce_scatter | solution.py:97
  19.2 13.1 %collective-permute-start = (bf16[128,1024]{1,0:T(8,128)(2,1)S(1)}, bf16[128,1024]{1,0:T(8,128)(2,1)S(1)}, u32[]{:S(2)}, u32[]{:S(2)}) collective-permute-start(bf16[128,1024]{1,0:T(8,128)(2,1)S(1)} %get-tuple-element.4), channel_id=1, source_target_pairs={{0,1},{1,2},{2,3},{3,4},{4,5},{5,6},{6,7},{7,0},{8,9},{9,10},{10,1... | collective-permute-start | bytes 786440 | tf_op jit(solution)/shard_map/ppermute | solution.py:52
  32.2 6.7 %collective-permute-start.1 = (bf16[128,1024]{1,0:T(8,128)(2,1)S(1)}, bf16[128,1024]{1,0:T(8,128)(2,1)S(1)}, u32[]{:S(2)}, u32[]{:S(2)}) collective-permute-start(bf16[128,1024]{1,0:T(8,128)(2,1)S(1)} %collective-permute-done), channel_id=1, source_target_pairs={{0,1},{1,2},{2,3},{3,4},{4,5},{5,6},{6,7},{7,0},{8,9},{9,10},{10,1... | collective-permute-start | bytes 786440 | tf_op jit(solution)/shard_map/ppermute | solution.py:52
  39.0 7.7 %collective-permute-start.2 = (bf16[128,1024]{1,0:T(8,128)(2,1)S(1)}, bf16[128,1024]{1,0:T(8,128)(2,1)S(1)}, u32[]{:S(2)}, u32[]{:S(2)}) collective-permute-start(bf16[128,1024]{1,0:T(8,128)(2,1)S(1)} %collective-permute-done.1), channel_id=1, source_target_pairs={{0,1},{1,2},{2,3},{3,4},{4,5},{5,6},{6,7},{7,0},{8,9},{9,10},{10,1... | collective-permute-start | bytes 786440 | tf_op jit(solution)/shard_map/ppermute | solution.py:52
  46.6 6.7 %collective-permute-start.3 = (bf16[128,1024]{1,0:T(8,128)(2,1)S(1)}, bf16[128,1024]{1,0:T(8,128)(2,1)S(1)}, u32[]{:S(2)}, u32[]{:S(2)}) collective-permute-start(bf16[128,1024]{1,0:T(8,128)(2,1)S(1)} %collective-permute-done.2), channel_id=1, source_target_pairs={{0,1},{1,2},{2,3},{3,4},{4,5},{5,6},{6,7},{7,0},{8,9},{9,10},{10,1... | collective-permute-start | bytes 786440 | tf_op jit(solution)/shard_map/ppermute | solution.py:52
  53.3 6.7 %collective-permute-start.4 = (bf16[128,1024]{1,0:T(8,128)(2,1)S(1)}, bf16[128,1024]{1,0:T(8,128)(2,1)S(1)}, u32[]{:S(2)}, u32[]{:S(2)}) collective-permute-start(bf16[128,1024]{1,0:T(8,128)(2,1)S(1)} %collective-permute-done.3), channel_id=1, source_target_pairs={{0,1},{1,2},{2,3},{3,4},{4,5},{5,6},{6,7},{7,0},{8,9},{9,10},{10,1... | collective-permute-start | bytes 786440 | tf_op jit(solution)/shard_map/ppermute | solution.py:52
  60.0 6.7 %collective-permute-start.5 = (bf16[128,1024]{1,0:T(8,128)(2,1)S(1)}, bf16[128,1024]{1,0:T(8,128)(2,1)S(1)}, u32[]{:S(2)}, u32[]{:S(2)}) collective-permute-start(bf16[128,1024]{1,0:T(8,128)(2,1)S(1)} %collective-permute-done.4), channel_id=1, source_target_pairs={{0,1},{1,2},{2,3},{3,4},{4,5},{5,6},{6,7},{7,0},{8,9},{9,10},{10,1... | collective-permute-start | bytes 786440 | tf_op jit(solution)/shard_map/ppermute | solution.py:52
  66.7 6.7 %collective-permute-start.6 = (bf16[128,1024]{1,0:T(8,128)(2,1)S(1)}, bf16[128,1024]{1,0:T(8,128)(2,1)S(1)}, u32[]{:S(2)}, u32[]{:S(2)}) collective-permute-start(bf16[128,1024]{1,0:T(8,128)(2,1)S(1)} %collective-permute-done.5), channel_id=1, source_target_pairs={{0,1},{1,2},{2,3},{3,4},{4,5},{5,6},{6,7},{7,0},{8,9},{9,10},{10,1... | collective-permute-start | bytes 786440 | tf_op jit(solution)/shard_map/ppermute | solution.py:52
  81.1 14.0 %copy-start.4 = (f32[128,1024]{1,0:T(8,128)S(1)}, f32[128,1024]{1,0:T(8,128)}, u32[]{:S(2)}) copy-start(f32[128,1024]{1,0:T(8,128)} %fusion.6) | copy-start | bytes 1572868
  81.6 14.0 %copy-start.5 = (bf16[512,1024]{1,0:T(8,128)(2,1)S(1)}, bf16[512,1024]{1,0:T(8,128)(2,1)}, u32[]{:S(2)}) copy-start(bf16[512,1024]{1,0:T(8,128)(2,1)} %all-gather.9.cloned.1.call-done) | copy-start | bytes 3145732
  100.3 85.8 %reduce-scatter.4.cloned.1.call-start = ((), (), s32[]{:S(2)}) async-start(), calls=%async_computation.4 | async-start | bytes 2621440 | tf_op jit(solution)/shard_map/reduce_scatter | solution.py:89
  104.5 135.1 %all-gather.11.cloned.1.call-start = ((), (), s32[]{:S(2)}) async-start(), calls=%async_computation.8 | async-start | bytes 4718592 | tf_op jit(solution)/shard_map/all_gather | solution.py:108
  188.6 0.7 copy-start.2
  188.6 2.3 copy-start.1
  190.1 98.0 %reduce-scatter.8.cloned.1.call-start = ((), (), s32[]{:S(2)}) async-start(), calls=%async_computation.6 | async-start | bytes 2621440 | tf_op jit(solution)/shard_map/reduce_scatter | solution.py:112
  246.1 7.3 %copy-start.3 = (bf16[128,1024]{1,0:T(8,128)(2,1)S(1)}, bf16[128,1024]{1,0:T(8,128)(2,1)}, u32[]{:S(2)}) copy-start(bf16[128,1024]{1,0:T(8,128)(2,1)} %copy-done.2) | copy-start | bytes 786436
Sparse Core Ops, SparseCore 0:
  13.2 30.7 all-gather.8
  100.4 39.7 reduce-scatter.5
  142.5 43.5 reduce-scatter.3
  190.3 49.2 all-gather.10
  246.2 41.8 reduce-scatter.7
